TPU v7x, 32 devices: a whole 2x2x4 slice. The times are simulated.
32 devices in a mesh: groups: 2 (over x), seq: 8 (over z, y), rep: 2 (over core).
Axes of the slice: x: 2, y: 2, z: 4, core: 2. Of those that a mesh axis runs over, the one named last changes fastest.
Arguments:
- inputs: bfloat16 [4, 4096, 1536], P(('groups', 'rep'), 'seq'), parts along dimension 0, may hold values from -6 to 6
- lengths: int32 [4], P(('groups', 'rep')), parts along dimension 0, may hold values from 2049 to 4096, as said below
- conv_weight: bfloat16 [3, 48, 1536], replicated, may hold values from -0.5 to 0.5
- point_weight: bfloat16 [1536, 1536], replicated, may hold values from -0.15625 to 0.15625
- cotangent: bfloat16 [4, 4096, 1536], P(('groups', 'rep'), 'seq'), parts along dimension 0, may hold values from -6 to 6
Outputs:
- output: bfloat16 [4, 4096, 1536], P(('groups', 'rep'), 'seq'), parts along dimension 0
- grad_inputs: bfloat16 [4, 4096, 1536], P(('groups', 'rep'), 'seq'), parts along dimension 0
- grad_point: float32 [3072, 1536], P(('groups', 'seq', 'rep')), parts along dimension 0
- grad_conv: float32 [6, 48, 1536], P('groups'), parts along dimension 0
There are 2 independent parts, one for each index of `groups`. A program takes and returns all parts, laid end to end along the dimension named above; an argument that names none is the same for every part. Nothing has to cross between parts.
Inputs may be any that keep to these rules, and one draw needn't show every extreme that they name: `lengths`: one sample in each draw has all 4096 bins valid.
All inputs are finite; a program needn't handle non-finite values.
Results may differ from a plain program's by a relative error of at most 0.0031.
Values may be sent and summed in bfloat16 or wider, within the bound.
No kernel may reach another device: no remote copies, remote signals or barrier semaphores. Data moves between devices by JAX's collectives and lax.ppermute only.
A program may use at most 128 MiB of HBM per device.

v0:
```python
import math
import jax
import jax.numpy as jnp
from jax import lax
from jax.sharding import PartitionSpec as P

GROUP_CHANNELS = 48
DILATION_STEP = 64


def with_halo(cells, sides, width):
    for axis, dim in sides:
        count = lax.axis_size(axis)
        ends = count - 1
        head = lax.slice_in_dim(cells, 0, width, axis=dim)
        tail = lax.slice_in_dim(cells, cells.shape[dim] - width, cells.shape[dim], axis=dim)
        cells = jnp.concatenate(
            [
                lax.ppermute(tail, axis, [(i, (i + 1) % count) for i in range(ends)]),
                cells,
                lax.ppermute(head, axis, [((i + 1) % count, i) for i in range(ends)]),
            ],
            axis=dim,
        )
    return cells


def gelu_pair(pre):
    cdf = 0.5 * (1.0 + jax.scipy.special.erf(pre * 0.7071067811865476))
    dens = jnp.exp(-0.5 * pre * pre) * 0.3989422804014327
    return (pre * cdf, cdf + pre * dens)


def conv_taps(padded_input, weight, sequence_length):
    group_count = weight.shape[2] // GROUP_CHANNELS
    total = jnp.zeros(
        (padded_input.shape[0], sequence_length, group_count, GROUP_CHANNELS), jnp.float32
    )
    for kernel_offset in range(3):
        segment_window = padded_input[
            :, kernel_offset * DILATION_STEP : kernel_offset * DILATION_STEP + sequence_length
        ].reshape(padded_input.shape[0], sequence_length, group_count, GROUP_CHANNELS)
        wk = weight[kernel_offset].reshape(GROUP_CHANNELS, group_count, GROUP_CHANNELS)
        total = total + jnp.einsum(
            "slgi,igj->slgj", segment_window, wk, preferred_element_type=jnp.float32
        )
    return total.reshape(padded_input.shape[0], sequence_length, group_count * GROUP_CHANNELS)


def transpose_taps(padded_input, weight, sequence_length):
    group_count = weight.shape[2] // GROUP_CHANNELS
    total = jnp.zeros(
        (padded_input.shape[0], sequence_length, group_count, GROUP_CHANNELS), jnp.float32
    )
    for kernel_offset in range(3):
        segment_window = padded_input[
            :,
            (2 - kernel_offset) * DILATION_STEP : (2 - kernel_offset) * DILATION_STEP
            + sequence_length,
        ].reshape(padded_input.shape[0], sequence_length, group_count, GROUP_CHANNELS)
        wk = weight[kernel_offset].reshape(GROUP_CHANNELS, group_count, GROUP_CHANNELS)
        total = total + jnp.einsum(
            "slgj,igj->slgi", segment_window, wk, preferred_element_type=jnp.float32
        )
    return total.reshape(padded_input.shape[0], sequence_length, group_count * GROUP_CHANNELS)


def weight_taps(input_padded, output_gradient, sequence_length):
    group_count = output_gradient.shape[2] // GROUP_CHANNELS
    grouped = output_gradient.reshape(
        output_gradient.shape[0], sequence_length, group_count, GROUP_CHANNELS
    )
    taps = []
    for kernel_offset in range(3):
        segment_window = input_padded[
            :, kernel_offset * DILATION_STEP : kernel_offset * DILATION_STEP + sequence_length
        ].reshape(output_gradient.shape[0], sequence_length, group_count, GROUP_CHANNELS)
        taps.append(
            jnp.einsum(
                "slgi,slgj->igj", segment_window, grouped, preferred_element_type=jnp.float32
            ).reshape(GROUP_CHANNELS, group_count * GROUP_CHANNELS)
        )
    return jnp.stack(taps)


def on_device(inputs, lengths, conv_weight, point_weight, cotangent):
    local_bins = inputs.shape[1]
    chans = inputs.shape[2]
    seq_count = lax.axis_size("seq")
    rep_count = lax.axis_size("rep")
    seq_index = lax.axis_index("seq")
    positions = seq_index * local_bins + jnp.arange(local_bins, dtype=jnp.int32)
    mask = (positions[None, :] < lengths[:, None]).astype(jnp.float32)
    mask3 = mask[:, :, None]
    masked_input = (inputs.astype(jnp.float32) * mask3).astype(jnp.bfloat16)
    scale = 1.0 / math.sqrt(rep_count * seq_count * local_bins)
    padded_input = with_halo(masked_input, (("seq", 1),), DILATION_STEP)
    pre = conv_taps(padded_input, conv_weight, local_bins)
    act_val, slope = gelu_pair(pre)
    act = (act_val * mask3).astype(jnp.bfloat16)
    act_rows = act.reshape(local_bins, chans)
    cot_rows = cotangent.reshape(local_bins, chans)
    proj = jnp.dot(act_rows, point_weight, preferred_element_type=jnp.float32).reshape(inputs.shape)
    output = (inputs.astype(jnp.float32) + proj).astype(jnp.bfloat16)
    back = lax.dot_general(
        cot_rows, point_weight, (((1,), (1,)), ((), ())), preferred_element_type=jnp.float32
    )
    preactivation_gradient = (back.reshape(inputs.shape) * slope * mask3).astype(jnp.bfloat16)
    padded_gradient = with_halo(preactivation_gradient, (("seq", 1),), DILATION_STEP)
    spread = transpose_taps(padded_gradient, conv_weight, local_bins)
    conv_local = weight_taps(padded_input, preactivation_gradient, local_bins)
    grad_conv = lax.psum(conv_local, ("seq", "rep")) * scale
    grad_inputs = (cotangent.astype(jnp.float32) + mask3 * spread).astype(jnp.bfloat16)
    grad_point = lax.psum_scatter(
        lax.dot_general(
            act_rows, cot_rows, (((0,), (0,)), ((), ())), preferred_element_type=jnp.float32
        ),
        ("seq", "rep"),
        scatter_dimension=0,
        tiled=True,
    )
    grad_point = grad_point * scale
    return (output, grad_inputs, grad_point, grad_conv)


def solution(mesh):
    return jax.shard_map(
        on_device,
        mesh=mesh,
        in_specs=(
            P(("groups", "rep"), "seq", None),
            P(("groups", "rep")),
            P(),
            P(),
            P(("groups", "rep"), "seq", None),
        ),
        out_specs=(
            P(("groups", "rep"), "seq", None),
            P(("groups", "rep"), "seq", None),
            P(("groups", "seq", "rep"), None),
            P("groups", None, None),
        ),
        check_vma=False,
    )
```

profile of v0, /device:TPU:0, one launch (start us, length us, event | category | flops | bytes accessed | tf_op | source)
XLA Modules:
  0.0 282.3 jit_solution(17731582967760469702)
XLA Ops:
  7.2 0.0 all-reduce.2.cloned.1.call-start
  7.9 1.7 fusion.1
  9.6 0.8 fusion.21
  10.4 1.3 collective-permute-start.1
  11.7 6.2 %collective-permute-start = (bf16[1,64,1536]{2,1,0:T(8,128)(2,1)}, bf16[1,64,1536]{2,1,0:T(8,128)(2,1)}, u32[]{:S(2)}, u32[]{:S(2)}) collective-permute-start(bf16[1,64,1536]{2,1,0:T(8,128)(2,1)} %get-tuple-element.11), channel_id=1, source_target_pairs={{0,2},{2,4},{4,6},{6,8},{8,10},{10,12},{12,14},{1,3},{3,5},{5,7},{... | collective-permute-start | bytes 589832 | tf_op jit(solution)/shard_map/ppermute | solution.py:19
  17.8 0.7 copy.36
  18.6 1.8 fusion.22
  20.4 1.1 copy.39
  21.5 1.8 copy.35
  23.3 1.8 copy.37
  25.2 3.2 %fusion.29 = f32[32,512,48]{1,2,0:T(8,128)} fusion(bf16[48,32,48]{0,2,1:T(8,128)(2,1)} %bitcast.90, bf16[512,32,48]{0,2,1:T(8,128)(2,1)S(1)} %bitcast.73), kind=kOutput, calls=%fused_computation.48 | convolution fusion | flops 75497472 | bytes 4866048 | tf_op jit(solution)/shard_map/slgi,igj->slgj/dot_general | solution.py:44
  28.4 2.9 %pad_maximum_fusion.2 = (bf16[1,512,1536]{2,1,0:T(8,128)(2,1)}, bf16[1,512,1536]{2,1,0:T(8,128)(2,1)}) fusion(bf16[1,64,1536]{2,1,0:T(8,128)(2,1)} %collective-permute-done.1, bf16[1,512,1536]{2,1,0:T(8,128)(2,1)S(1)} %fusion.1, bf16[1,64,1536]{2,1,0:T(8,128)(2,1)} %collective-permute-done), kind=kLoop, calls=%fused_computation.21 | loop fusion | flops 6291456 | bytes 5111808 | tf_op jit(solution)/shard_map/concatenate | solution.py:17
  31.3 2.6 copy.38
  33.9 1.7 copy.34
  35.7 2.0 fusion.28
  37.6 0.1 copy-done.2
  37.7 1.0 copy-done.4
  38.7 2.2 add_add_fusion.1
  40.9 3.7 %copy.41 = f32[512,1536]{1,0:T(8,128)} copy(f32[512,1536]{0,1:T(8,128)} %bitcast.79) | data formatting | bytes 6291456 | tf_op jit(solution)/shard_map/reshape | solution.py:47
  44.6 7.0 %fusion.7 = bf16[512,1536]{1,0:T(8,128)(2,1)} fusion(f32[512,1536]{1,0:T(8,128)} %copy.41, bf16[1536,1536]{1,0:T(8,128)(2,1)} %param.8, bf16[1,512,1536]{2,1,0:T(8,128)(2,1)S(1)} %copy-done.10, f32[512]{0:T(512)S(1)} %fusion.16), kind=kOutput, calls=%fused_computation.18 | convolution fusion | flops 2424569856 | bytes 11012096 | tf_op jit(solution)/shard_map/dot_general | solution.py:105
  51.5 1.7 copy.47
  53.3 3.0 %fusion.27 = f32[32,48,48]{2,1,0:T(8,128)} fusion(bf16[512,32,48]{0,2,1:T(8,128)(2,1)S(1)} %bitcast.69, bf16[512,32,48]{0,2,1:T(8,128)(2,1)} %bitcast.77), kind=kOutput, calls=%fused_computation.46 | convolution fusion | flops 75497472 | bytes 3440640 | tf_op jit(solution)/shard_map/slgi,slgj->igj/dot_general | solution.py:79
  56.2 1.4 fusion.26
  57.7 1.5 fusion.25
  59.1 2.1 copy.52
  61.2 1.0 copy.53
  62.2 0.2 copy.54
  62.4 2.0 pad_maximum_fusion.4
  64.5 0.0 reduce-scatter.2.cloned.1.call-start
  64.5 8.6 %fusion.8 = f32[1536,1536]{1,0:T(8,128)} fusion(bf16[1,512,1536]{2,1,0:T(8,128)(2,1)} %param.9, f32[1,512,1,1,1,1,1536]{1,6,5,4,3,2,0:T(8,128)} %bitcast.80, f32[512]{0:T(512)S(1)} %fusion.16), kind=kOutput, calls=%fused_computation.23 | convolution fusion | flops 2420637696 | bytes 14157824 | tf_op jit(solution)/shard_map/dot_general | solution.py:115
  73.2 1.4 copy-done.5
  74.6 4.2 %collective-permute-start.3 = (bf16[1,64,1536]{2,1,0:T(8,128)(2,1)S(1)}, bf16[1,64,1536]{2,1,0:T(8,128)(2,1)S(1)}, u32[]{:S(2)}, u32[]{:S(2)}) collective-permute-start(bf16[1,64,1536]{2,1,0:T(8,128)(2,1)S(1)} %get-tuple-element.6), channel_id=1, source_target_pairs={{0,2},{2,4},{4,6},{6,8},{8,10},{10,12},{12,14},{1,3},{3,5},{5,7},{... | collective-permute-start | bytes 589832 | tf_op jit(solution)/shard_map/ppermute | solution.py:19
  78.8 1.6 collective-permute-start.2
  80.4 7.6 %fusion.2 = bf16[1,512,1536]{2,1,0:T(8,128)(2,1)} fusion(bf16[1,512,1536]{2,1,0:T(8,128)(2,1)} %param.5, bf16[1536,1536]{1,0:T(8,128)(2,1)} %param.8, f32[512,1536]{1,0:T(8,128)} %copy.41, f32[512]{0:T(512)S(1)} %fusion.16), kind=kOutput, calls=%fused_computation.7 | convolution fusion | flops 2422996992 | bytes 11012096 | tf_op jit(solution)/shard_map/dot_general | solution.py:103
  88.0 2.3 fusion.24
  90.3 1.4 pad_maximum_fusion
  91.7 2.6 copy.49
  94.3 0.7 copy.45
  95.0 1.8 fusion.23
  96.8 0.2 copy-done.3
  97.0 0.5 copy-done.6
  97.5 2.3 add_add_fusion
  99.8 2.4 copy.51
  102.1 3.0 %add_convert_fusion = bf16[1,512,1536]{2,1,0:T(8,128)(2,1)} fusion(f32[1,512,1536]{2,1,0:T(8,128)S(1)} %copy.51, bf16[1,512,1536]{2,1,0:T(8,128)(2,1)} %param.9, f32[512]{0:T(512)S(1)} %fusion.16), kind=kLoop, calls=%fused_computation.13 | loop fusion | flops 3145728 | bytes 6293504 | tf_op jit(solution)/shard_map/convert_element_type | solution.py:113
  105.1 53.9 %all-reduce.2.cloned.1.call-done = f32[3,48,1536]{2,1,0:T(8,128)} async-done(((f32[3,48,1536]{2,1,0:T(8,128)}), f32[3,48,1536]{2,1,0:T(8,128)}) %all-reduce.2.cloned.1.call-update) | async-done | bytes 884752 | tf_op jit(solution)/shard_map/psum | solution.py:112
  159.1 2.2 broadcast_multiply_fusion
  161.2 112.3 %reduce-scatter.2.cloned.1.call-done = f32[96,1536]{1,0:T(8,128)} async-done(((f32[1536,1536]{1,0:T(8,128)}), f32[96,1536]{1,0:T(8,128)}) %reduce-scatter.2.cloned.1.call-update) | async-done | bytes 589840 | tf_op jit(solution)/shard_map/reduce_scatter | solution.py:114
  273.5 1.9 broadcast_multiply_fusion.1
  (25 shorter events, 0.1 us)
Async XLA Ops:
  7.2 151.9 %all-reduce.2.cloned.1.call-start = ((), (), s32[]{:S(2)}) async-start(), calls=%async_computation.2 | async-start | bytes 1769472 | tf_op jit(solution)/shard_map/psum | solution.py:112
  10.4 18.0 %collective-permute-start.1 = (bf16[1,64,1536]{2,1,0:T(8,128)(2,1)}, bf16[1,64,1536]{2,1,0:T(8,128)(2,1)}, u32[]{:S(2)}, u32[]{:S(2)}) collective-permute-start(bf16[1,64,1536]{2,1,0:T(8,128)(2,1)} %get-tuple-element.10), channel_id=1, source_target_pairs={{2,0},{4,2},{6,4},{8,6},{10,8},{12,10},{14,12},{3,1},{5,3},{7,5},{... | collective-permute-start | bytes 589832 | tf_op jit(solution)/shard_map/ppermute | solution.py:21
  11.7 16.7 %collective-permute-start = (bf16[1,64,1536]{2,1,0:T(8,128)(2,1)}, bf16[1,64,1536]{2,1,0:T(8,128)(2,1)}, u32[]{:S(2)}, u32[]{:S(2)}) collective-permute-start(bf16[1,64,1536]{2,1,0:T(8,128)(2,1)} %get-tuple-element.11), channel_id=1, source_target_pairs={{0,2},{2,4},{4,6},{6,8},{8,10},{10,12},{12,14},{1,3},{3,5},{5,7},{... | collective-permute-start | bytes 589832 | tf_op jit(solution)/shard_map/ppermute | solution.py:19
  35.6 5.3 %copy-start = (bf16[1,512,1536]{1,2,0:T(8,128)(2,1)}, bf16[1,512,1536]{1,2,0:T(8,128)(2,1)S(1)}, u32[]{:S(2)}) copy-start(bf16[1,512,1536]{1,2,0:T(8,128)(2,1)S(1)} %copy.34) | copy-start | bytes 4718596
  35.6 2.1 copy-start.2
  35.6 3.0 %copy-start.4 = (f32[32,512,48]{1,2,0:T(8,128)S(1)}, f32[32,512,48]{1,2,0:T(8,128)}, u32[]{:S(2)}) copy-start(f32[32,512,48]{1,2,0:T(8,128)} %fusion.29) | copy-start | bytes 9437188
  40.9 3.7 %copy-start.10 = (bf16[1,512,1536]{2,1,0:T(8,128)(2,1)S(1)}, bf16[1,512,1536]{2,1,0:T(8,128)(2,1)}, u32[]{:S(2)}) copy-start(bf16[1,512,1536]{2,1,0:T(8,128)(2,1)} %param.9) | copy-start | bytes 4718596
  53.3 4.4 %copy-start.1 = (bf16[1,512,1536]{1,2,0:T(8,128)(2,1)S(1)}, bf16[1,512,1536]{1,2,0:T(8,128)(2,1)}, u32[]{:S(2)}) copy-start(bf16[1,512,1536]{1,2,0:T(8,128)(2,1)} %copy-done) | copy-start | bytes 4718596
  57.7 3.5 %copy-start.9 = (f32[32,48,48]{2,1,0:T(8,128)S(1)}, f32[32,48,48]{2,1,0:T(8,128)}, u32[]{:S(2)}) copy-start(f32[32,48,48]{2,1,0:T(8,128)} %fusion.26) | copy-start | bytes 884740
  57.7 4.5 %copy-start.8 = (f32[32,48,48]{2,1,0:T(8,128)S(1)}, f32[32,48,48]{2,1,0:T(8,128)}, u32[]{:S(2)}) copy-start(f32[32,48,48]{2,1,0:T(8,128)} %fusion.27) | copy-start | bytes 884740
  64.5 209.1 %reduce-scatter.2.cloned.1.call-start = ((), (), s32[]{:S(2)}) async-start(), calls=%async_computation.1 | async-start | bytes 10027008 | tf_op jit(solution)/shard_map/reduce_scatter | solution.py:114
  73.2 1.4 copy-start.5
  74.6 15.7 %collective-permute-start.3 = (bf16[1,64,1536]{2,1,0:T(8,128)(2,1)S(1)}, bf16[1,64,1536]{2,1,0:T(8,128)(2,1)S(1)}, u32[]{:S(2)}, u32[]{:S(2)}) collective-permute-start(bf16[1,64,1536]{2,1,0:T(8,128)(2,1)S(1)} %get-tuple-element.6), channel_id=1, source_target_pairs={{0,2},{2,4},{4,6},{6,8},{8,10},{10,12},{12,14},{1,3},{3,5},{5,7},{... | collective-permute-start | bytes 589832 | tf_op jit(solution)/shard_map/ppermute | solution.py:19
  78.8 9.2 %copy-start.7 = (bf16[1,48,1536]{1,2,0:T(8,128)(2,1)S(1)}, bf16[1,48,1536]{1,2,0:T(8,128)(2,1)}, u32[]{:S(2)}) copy-start(bf16[1,48,1536]{1,2,0:T(8,128)(2,1)} %copy.37) | copy-start | bytes 442372
  78.8 11.5 %collective-permute-start.2 = (bf16[1,64,1536]{2,1,0:T(8,128)(2,1)S(1)}, bf16[1,64,1536]{2,1,0:T(8,128)(2,1)S(1)}, u32[]{:S(2)}, u32[]{:S(2)}) collective-permute-start(bf16[1,64,1536]{2,1,0:T(8,128)(2,1)S(1)} %get-tuple-element.7), channel_id=1, source_target_pairs={{2,0},{4,2},{6,4},{8,6},{10,8},{12,10},{14,12},{3,1},{5,3},{7,5},{... | collective-permute-start | bytes 589832 | tf_op jit(solution)/shard_map/ppermute | solution.py:21
  95.0 2.0 copy-start.3
  95.0 2.5 copy-start.6
Sparse Core Ops, SparseCore 0:
  64.6 94.4 all-reduce.1
  163.2 110.3 reduce-scatter.1
where the time goes:
time: 283 us; the launch traced here: 282 us
  waiting for transfers between devices  166 us (59%)
  matrix products  42.8 us (15%)
  local copies, waits for them, and re-layouts  29.9 us (11%)
  other arithmetic  15.1 us (5%)
  between operations  14.9 us (5%)
  starting transfers between devices  13.3 us (5%)
    reduce_scatter x1, waiting for transfers between devices, on_device(): lax.psum_scatter(lax.dot_general(act_rows, cot_rows, (((0,), (0,)), ((),...  112 us
    psum x1, waiting for transfers between devices, on_device(): grad_conv = lax.psum(conv_local, ('seq', 'rep')) * scale  53.9 us
    ppermute x2, starting transfers between devices, with_halo(): lax.ppermute(tail, axis, [(i, (i + 1) % count) for i in range(ends)])  10.4 us
    dot_general x1, matrix products, on_device(): lax.dot_general(act_rows, cot_rows, (((0,), (0,)), ((), ())), preferred_e...  8.65 us
    dot_general x1, matrix products, on_device(): jnp.dot(act_rows, point_weight, preferred_element_type=jnp.float32)  7.61 us
    dot_general x3, matrix products, conv_taps(): jnp.einsum('slgi,igj->slgj', segment_window, wk, preferred_element_type=j...  7.38 us
    dot_general x1, matrix products, on_device(): lax.dot_general(cot_rows, point_weight, (((1,), (1,)), ((), ())), preferr...  6.98 us
    slice x4, local copies, waits for them, and re-layouts, conv_taps(): weight[kernel_offset].reshape(GROUP_CHANNELS, group_count, GROUP_CHANNELS)  6.61 us
  transfers between devices with their start and end apart: 6, of which 2 were waited for; matrix products, arithmetic and copies ran while one was open for 16% of the time, Pallas kernels for 0%

commit v1 on v0

--- a/solution.py
+++ b/solution.py
@@ -109,7 +109,7 @@
     padded_gradient = with_halo(preactivation_gradient, (("seq", 1),), DILATION_STEP)
     spread = transpose_taps(padded_gradient, conv_weight, local_bins)
     conv_local = weight_taps(padded_input, preactivation_gradient, local_bins)
-    grad_conv = lax.psum(conv_local, ("seq", "rep")) * scale
+    grad_conv = lax.psum(lax.psum(conv_local, "rep"), "seq") * scale
     grad_inputs = (cotangent.astype(jnp.float32) + mask3 * spread).astype(jnp.bfloat16)
     grad_point = lax.psum_scatter(
         lax.dot_general(

time: 283 us -> 222 us (0.78)
  waiting for transfers between devices: 166 us -> 102 us
    reduce_scatter x1, waiting for transfers between devices: 112 us -> 10.3 us  [on_device(): lax.psum_scatter(lax.dot_general(act_rows, cot_rows, (((0,), (0,)), ((),...]
    psum x1 -> x2, waiting for transfers between devices: 53.9 us -> 92 us  [on_device(): grad_conv = lax.psum(lax.psum(conv_local, 'rep'), 'seq') * scale]
  transfers between devices with their start and end apart: 6 -> 7, of which waited for: 2 -> 3; matrix products, arithmetic and copies ran while one was open for 16% -> 21% of each run, Pallas kernels for 0% -> 0%
where the time goes in v1:
time: 222 us; the launch traced here: 221 us
  waiting for transfers between devices  102 us (46%)
  matrix products  43.2 us (19%)
  local copies, waits for them, and re-layouts  31.1 us (14%)
  between operations  16.3 us (7%)
  other arithmetic  15.4 us (7%)
  starting transfers between devices  12.9 us (6%)
    psum x2, waiting for transfers between devices, on_device(): grad_conv = lax.psum(lax.psum(conv_local, 'rep'), 'seq') * scale  92 us
    reduce_scatter x1, waiting for transfers between devices, on_device(): lax.psum_scatter(lax.dot_general(act_rows, cot_rows, (((0,), (0,)), ((),...  10.3 us
    ppermute x2, starting transfers between devices, with_halo(): lax.ppermute(tail, axis, [(i, (i + 1) % count) for i in range(ends)])  9.85 us
    dot_general x1, matrix products, on_device(): jnp.dot(act_rows, point_weight, preferred_element_type=jnp.float32)  8.41 us
    dot_general x1, matrix products, on_device(): lax.dot_general(act_rows, cot_rows, (((0,), (0,)), ((), ())), preferred_e...  8.21 us
    dot_general x3, matrix products, conv_taps(): jnp.einsum('slgi,igj->slgj', segment_window, wk, preferred_element_type=j...  7.37 us
    dot_general x1, matrix products, on_device(): lax.dot_general(cot_rows, point_weight, (((1,), (1,)), ((), ())), preferr...  6.99 us
    slice x4, local copies, waits for them, and re-layouts, conv_taps(): weight[kernel_offset].reshape(GROUP_CHANNELS, group_count, GROUP_CHANNELS)  6.62 us
  transfers between devices with their start and end apart: 7, of which 3 were waited for; matrix products, arithmetic and copies ran while one was open for 21% of the time, Pallas kernels for 0%

profile of v1, /device:TPU:0, one launch (start us, length us, event | category | flops | bytes accessed | tf_op | source)
XLA Modules:
  0.0 221.2 jit_solution(1034440676623830432)
XLA Ops:
  8.7 1.7 fusion.1
  10.4 0.8 fusion.21
  11.2 1.3 collective-permute-start.1
  12.5 6.2 %collective-permute-start = (bf16[1,64,1536]{2,1,0:T(8,128)(2,1)}, bf16[1,64,1536]{2,1,0:T(8,128)(2,1)}, u32[]{:S(2)}, u32[]{:S(2)}) collective-permute-start(bf16[1,64,1536]{2,1,0:T(8,128)(2,1)} %get-tuple-element.11), channel_id=1, source_target_pairs={{0,2},{2,4},{4,6},{6,8},{8,10},{10,12},{12,14},{1,3},{3,5},{5,7},{... | collective-permute-start | bytes 589832 | tf_op jit(solution)/shard_map/ppermute | solution.py:19
  18.7 0.7 copy.36
  19.4 1.8 fusion.22
  21.2 1.1 copy.39
  22.3 1.8 copy.35
  24.2 1.8 copy.37
  26.0 3.2 %fusion.29 = f32[32,512,48]{1,2,0:T(8,128)} fusion(bf16[48,32,48]{0,2,1:T(8,128)(2,1)} %bitcast.90, bf16[512,32,48]{0,2,1:T(8,128)(2,1)S(1)} %bitcast.73), kind=kOutput, calls=%fused_computation.48 | convolution fusion | flops 75497472 | bytes 4866048 | tf_op jit(solution)/shard_map/slgi,igj->slgj/dot_general | solution.py:44
  29.2 2.9 %pad_maximum_fusion.2 = (bf16[1,512,1536]{2,1,0:T(8,128)(2,1)}, bf16[1,512,1536]{2,1,0:T(8,128)(2,1)}) fusion(bf16[1,64,1536]{2,1,0:T(8,128)(2,1)} %collective-permute-done.1, bf16[1,512,1536]{2,1,0:T(8,128)(2,1)S(1)} %fusion.1, bf16[1,64,1536]{2,1,0:T(8,128)(2,1)} %collective-permute-done), kind=kLoop, calls=%fused_computation.21 | loop fusion | flops 6291456 | bytes 5111808 | tf_op jit(solution)/shard_map/concatenate | solution.py:17
  32.1 2.6 %copy.38 = bf16[1,512,1536]{1,2,0:T(8,128)(2,1)} copy(bf16[1,512,1536]{2,1,0:T(8,128)(2,1)} %get-tuple-element.8) | data formatting | bytes 3145728 | tf_op jit(solution)/shard_map/slice | solution.py:40
  34.7 1.7 copy.34
  36.5 2.0 fusion.28
  38.5 0.1 copy-done.2
  38.6 1.0 copy-done.4
  39.5 2.2 add_add_fusion.1
  41.7 3.7 %copy.41 = f32[512,1536]{1,0:T(8,128)} copy(f32[512,1536]{0,1:T(8,128)} %bitcast.79) | data formatting | bytes 6291456 | tf_op jit(solution)/shard_map/reshape | solution.py:47
  45.4 7.0 %fusion.7 = bf16[512,1536]{1,0:T(8,128)(2,1)} fusion(f32[512,1536]{1,0:T(8,128)} %copy.41, bf16[1536,1536]{1,0:T(8,128)(2,1)} %param.8, bf16[1,512,1536]{2,1,0:T(8,128)(2,1)S(1)} %copy-done.10, f32[512]{0:T(512)S(1)} %fusion.16), kind=kOutput, calls=%fused_computation.18 | convolution fusion | flops 2424569856 | bytes 11012096 | tf_op jit(solution)/shard_map/dot_general | solution.py:105
  52.4 1.7 copy.47
  54.1 3.0 %fusion.27 = f32[32,48,48]{2,1,0:T(8,128)} fusion(bf16[512,32,48]{0,2,1:T(8,128)(2,1)S(1)} %bitcast.69, bf16[512,32,48]{0,2,1:T(8,128)(2,1)} %bitcast.77), kind=kOutput, calls=%fused_computation.46 | convolution fusion | flops 75497472 | bytes 3440640 | tf_op jit(solution)/shard_map/slgi,slgj->igj/dot_general | solution.py:79
  57.1 1.4 fusion.26
  58.5 1.5 fusion.25
  60.0 2.1 copy.52
  62.0 1.0 copy.53
  63.0 1.0 copy.54
  64.0 2.2 %pad_maximum_fusion.4 = f32[3,48,1536]{2,1,0:T(8,128)} fusion(f32[1,48,1536]{2,1,0:T(8,128)} %copy.54, f32[1,48,1536]{2,1,0:T(8,128)} %copy.53, f32[1,48,1536]{2,1,0:T(8,128)} %copy.52), kind=kLoop, calls=%fused_computation.31 | loop fusion | flops 442368 | bytes 1769472 | tf_op jit(solution)/shard_map/stack | solution.py:83
  66.3 20.4 %all-reduce.3.cloned.1.call-done = f32[3,48,1536]{2,1,0:T(8,128)} async-done(((f32[3,48,1536]{2,1,0:T(8,128)}), f32[3,48,1536]{2,1,0:T(8,128)}) %all-reduce.3.cloned.1.call-update) | async-done | bytes 884752 | tf_op jit(solution)/shard_map/psum | solution.py:112
  86.7 0.0 reduce-scatter.2.cloned.1.call-start
  86.8 8.2 %fusion.8 = f32[1536,1536]{1,0:T(8,128)} fusion(bf16[1,512,1536]{2,1,0:T(8,128)(2,1)S(1)} %copy-done.11, f32[1,512,1,1,1,1,1536]{1,6,5,4,3,2,0:T(8,128)} %bitcast.80, f32[512]{0:T(512)S(1)} %fusion.16), kind=kOutput, calls=%fused_computation.23 | convolution fusion | flops 2420637696 | bytes 14157824 | tf_op jit(solution)/shard_map/dot_general | solution.py:115
  95.0 1.4 copy-done.5
  96.4 3.7 %collective-permute-start.3 = (bf16[1,64,1536]{2,1,0:T(8,128)(2,1)S(1)}, bf16[1,64,1536]{2,1,0:T(8,128)(2,1)S(1)}, u32[]{:S(2)}, u32[]{:S(2)}) collective-permute-start(bf16[1,64,1536]{2,1,0:T(8,128)(2,1)S(1)} %get-tuple-element.6), channel_id=1, source_target_pairs={{0,2},{2,4},{4,6},{6,8},{8,10},{10,12},{12,14},{1,3},{3,5},{5,7},{... | collective-permute-start | bytes 589832 | tf_op jit(solution)/shard_map/ppermute | solution.py:19
  100.1 1.6 collective-permute-start.2
  101.7 8.4 %fusion.2 = bf16[1,512,1536]{2,1,0:T(8,128)(2,1)} fusion(bf16[1,512,1536]{2,1,0:T(8,128)(2,1)} %param.5, bf16[1536,1536]{1,0:T(8,128)(2,1)} %param.8, f32[512,1536]{1,0:T(8,128)} %copy.41, f32[512]{0:T(512)S(1)} %fusion.16), kind=kOutput, calls=%fused_computation.7 | convolution fusion | flops 2422996992 | bytes 11012096 | tf_op jit(solution)/shard_map/dot_general | solution.py:103
  110.1 2.3 %fusion.24 = f32[32,512,48]{1,2,0:T(8,128)} fusion(bf16[512,32,48]{0,2,1:T(8,128)(2,1)S(1)} %bitcast.72, bf16[48,32,48]{0,2,1:T(8,128)(2,1)S(1)} %bitcast.91), kind=kOutput, calls=%fused_computation.43 | convolution fusion | flops 75497472 | bytes 4866048 | tf_op jit(solution)/shard_map/slgj,igj->slgi/dot_general | solution.py:62
  112.4 1.4 pad_maximum_fusion
  113.8 2.7 %copy.49 = bf16[1,512,1536]{1,2,0:T(8,128)(2,1)} copy(bf16[1,512,1536]{2,1,0:T(8,128)(2,1)} %get-tuple-element.4) | data formatting | bytes 3145728 | tf_op jit(solution)/shard_map/slice | solution.py:56
  116.5 0.7 copy.45
  117.2 1.8 fusion.23
  119.1 0.6 copy-done.3
  119.6 0.5 copy-done.6
  120.2 2.3 %add_add_fusion = f32[32,512,48]{1,2,0:T(8,128)} fusion(f32[32,512,48]{1,2,0:T(8,128)S(1)} %fusion.23, f32[32,512,48]{1,2,0:T(8,128)S(1)} %copy-done.3, bf16[512,32,48]{0,2,1:T(8,128)(2,1)S(1)} %bitcast.85, bf16[48,32,48]{0,2,1:T(8,128)(2,1)S(1)} %bitcast.87), kind=kOutput, calls=%fused_computation.14 | convolution fusion | flops 77070336 | bytes 11157504 | tf_op jit(solution)/shard_map/slgj,igj->slgi/dot_general | solution.py:62
  122.4 2.4 %copy.51 = f32[1,512,1536]{2,1,0:T(8,128)S(1)} copy(f32[1,512,1536]{1,2,0:T(8,128)} %bitcast.81) | data formatting | bytes 6291456 | tf_op jit(solution)/shard_map/reshape | solution.py:65
  124.8 3.0 %add_convert_fusion = bf16[1,512,1536]{2,1,0:T(8,128)(2,1)} fusion(f32[1,512,1536]{2,1,0:T(8,128)S(1)} %copy.51, bf16[1,512,1536]{2,1,0:T(8,128)(2,1)} %param.9, f32[512]{0:T(512)S(1)} %fusion.16), kind=kLoop, calls=%fused_computation.13 | loop fusion | flops 3145728 | bytes 6293504 | tf_op jit(solution)/shard_map/convert_element_type | solution.py:113
  127.8 71.6 %all-reduce.5.cloned.1.call-done = f32[3,48,1536]{2,1,0:T(8,128)} async-done(((f32[3,48,1536]{2,1,0:T(8,128)}), f32[3,48,1536]{2,1,0:T(8,128)}) %all-reduce.5.cloned.1.call-update) | async-done | bytes 884752 | tf_op jit(solution)/shard_map/psum | solution.py:112
  199.4 2.2 broadcast_multiply_fusion
  201.5 10.3 %reduce-scatter.2.cloned.1.call-done = f32[96,1536]{1,0:T(8,128)} async-done(((f32[1536,1536]{1,0:T(8,128)}), f32[96,1536]{1,0:T(8,128)}) %reduce-scatter.2.cloned.1.call-update) | async-done | bytes 589840 | tf_op jit(solution)/shard_map/reduce_scatter | solution.py:114
  211.8 1.9 broadcast_multiply_fusion.1
  (30 shorter events, 0.2 us)
Async XLA Ops:
  8.0 78.7 %all-reduce.3.cloned.1.call-start = ((), (), s32[]{:S(2)}) async-start(), calls=%async_computation.2 | async-start | bytes 1769472 | tf_op jit(solution)/shard_map/psum | solution.py:112
  11.2 18.0 %collective-permute-start.1 = (bf16[1,64,1536]{2,1,0:T(8,128)(2,1)}, bf16[1,64,1536]{2,1,0:T(8,128)(2,1)}, u32[]{:S(2)}, u32[]{:S(2)}) collective-permute-start(bf16[1,64,1536]{2,1,0:T(8,128)(2,1)} %get-tuple-element.10), channel_id=1, source_target_pairs={{2,0},{4,2},{6,4},{8,6},{10,8},{12,10},{14,12},{3,1},{5,3},{7,5},{... | collective-permute-start | bytes 589832 | tf_op jit(solution)/shard_map/ppermute | solution.py:21
  12.5 16.7 %collective-permute-start = (bf16[1,64,1536]{2,1,0:T(8,128)(2,1)}, bf16[1,64,1536]{2,1,0:T(8,128)(2,1)}, u32[]{:S(2)}, u32[]{:S(2)}) collective-permute-start(bf16[1,64,1536]{2,1,0:T(8,128)(2,1)} %get-tuple-element.11), channel_id=1, source_target_pairs={{0,2},{2,4},{4,6},{6,8},{8,10},{10,12},{12,14},{1,3},{3,5},{5,7},{... | collective-permute-start | bytes 589832 | tf_op jit(solution)/shard_map/ppermute | solution.py:19
  36.5 5.3 %copy-start = (bf16[1,512,1536]{1,2,0:T(8,128)(2,1)}, bf16[1,512,1536]{1,2,0:T(8,128)(2,1)S(1)}, u32[]{:S(2)}) copy-start(bf16[1,512,1536]{1,2,0:T(8,128)(2,1)S(1)} %copy.34) | copy-start | bytes 4718596
  36.5 2.1 copy-start.2
  36.5 3.0 %copy-start.4 = (f32[32,512,48]{1,2,0:T(8,128)S(1)}, f32[32,512,48]{1,2,0:T(8,128)}, u32[]{:S(2)}) copy-start(f32[32,512,48]{1,2,0:T(8,128)} %fusion.29) | copy-start | bytes 9437188
  41.7 3.7 %copy-start.10 = (bf16[1,512,1536]{2,1,0:T(8,128)(2,1)S(1)}, bf16[1,512,1536]{2,1,0:T(8,128)(2,1)}, u32[]{:S(2)}) copy-start(bf16[1,512,1536]{2,1,0:T(8,128)(2,1)} %param.9) | copy-start | bytes 4718596
  54.1 4.4 %copy-start.1 = (bf16[1,512,1536]{1,2,0:T(8,128)(2,1)S(1)}, bf16[1,512,1536]{1,2,0:T(8,128)(2,1)}, u32[]{:S(2)}) copy-start(bf16[1,512,1536]{1,2,0:T(8,128)(2,1)} %copy-done) | copy-start | bytes 4718596
  58.5 3.5 %copy-start.9 = (f32[32,48,48]{2,1,0:T(8,128)S(1)}, f32[32,48,48]{2,1,0:T(8,128)}, u32[]{:S(2)}) copy-start(f32[32,48,48]{2,1,0:T(8,128)} %fusion.26) | copy-start | bytes 884740
  58.5 4.5 %copy-start.8 = (f32[32,48,48]{2,1,0:T(8,128)S(1)}, f32[32,48,48]{2,1,0:T(8,128)}, u32[]{:S(2)}) copy-start(f32[32,48,48]{2,1,0:T(8,128)} %fusion.27) | copy-start | bytes 884740
  64.0 22.8 %copy-start.11 = (bf16[1,512,1536]{2,1,0:T(8,128)(2,1)S(1)}, bf16[1,512,1536]{2,1,0:T(8,128)(2,1)}, u32[]{:S(2)}) copy-start(bf16[1,512,1536]{2,1,0:T(8,128)(2,1)} %param.9) | copy-start | bytes 4718596
  66.2 133.1 %all-reduce.5.cloned.1.call-start = ((), (), s32[]{:S(2)}) async-start(), calls=%async_computation.3 | async-start | bytes 1769472 | tf_op jit(solution)/shard_map/psum | solution.py:112
  86.7 125.1 %reduce-scatter.2.cloned.1.call-start = ((), (), s32[]{:S(2)}) async-start(), calls=%async_computation.1 | async-start | bytes 10027008 | tf_op jit(solution)/shard_map/reduce_scatter | solution.py:114
  95.0 1.4 copy-start.5
  96.4 16.0 %collective-permute-start.3 = (bf16[1,64,1536]{2,1,0:T(8,128)(2,1)S(1)}, bf16[1,64,1536]{2,1,0:T(8,128)(2,1)S(1)}, u32[]{:S(2)}, u32[]{:S(2)}) collective-permute-start(bf16[1,64,1536]{2,1,0:T(8,128)(2,1)S(1)} %get-tuple-element.6), channel_id=1, source_target_pairs={{0,2},{2,4},{4,6},{6,8},{8,10},{10,12},{12,14},{1,3},{3,5},{5,7},{... | collective-permute-start | bytes 589832 | tf_op jit(solution)/shard_map/ppermute | solution.py:19
  100.1 10.0 %copy-start.7 = (bf16[1,48,1536]{1,2,0:T(8,128)(2,1)S(1)}, bf16[1,48,1536]{1,2,0:T(8,128)(2,1)}, u32[]{:S(2)}) copy-start(bf16[1,48,1536]{1,2,0:T(8,128)(2,1)} %copy.37) | copy-start | bytes 442372
  100.1 12.3 %collective-permute-start.2 = (bf16[1,64,1536]{2,1,0:T(8,128)(2,1)S(1)}, bf16[1,64,1536]{2,1,0:T(8,128)(2,1)S(1)}, u32[]{:S(2)}, u32[]{:S(2)}) collective-permute-start(bf16[1,64,1536]{2,1,0:T(8,128)(2,1)S(1)} %get-tuple-element.7), channel_id=1, source_target_pairs={{2,0},{4,2},{6,4},{8,6},{10,8},{12,10},{14,12},{3,1},{5,3},{7,5},{... | collective-permute-start | bytes 589832 | tf_op jit(solution)/shard_map/ppermute | solution.py:21
  117.2 2.4 %copy-start.3 = (f32[32,512,48]{1,2,0:T(8,128)S(1)}, f32[32,512,48]{1,2,0:T(8,128)}, u32[]{:S(2)}) copy-start(f32[32,512,48]{1,2,0:T(8,128)} %fusion.24) | copy-start | bytes 9437188
  117.2 2.9 %copy-start.6 = (bf16[1,512,1536]{1,2,0:T(8,128)(2,1)S(1)}, bf16[1,512,1536]{1,2,0:T(8,128)(2,1)}, u32[]{:S(2)}) copy-start(bf16[1,512,1536]{1,2,0:T(8,128)(2,1)} %copy.49) | copy-start | bytes 4718596
Sparse Core Ops, SparseCore 0:
  66.3 20.3 all-reduce.2
  90.6 108.7 all-reduce.4
Sparse Core Ops, SparseCore 1:
  95.1 116.7 reduce-scatter.1
